TPU v7x, 32 devices: a whole 2x2x4 slice. The times are simulated.
32 devices in a mesh: slab: 8 (over z, x), orient: 4 (over y, core).
Axes of the slice: x: 2, y: 2, z: 4, core: 2. Of those that a mesh axis runs over, the one named last changes fastest.
Arguments:
- tiles: bfloat16 [192, 1, 128, 128], P('slab'), may hold values from -8 to 8
- assigned_worker: int32 [192], P('slab'), may hold values from -1 to 7, as said below
- wedge_mask: int32 [128, 128], replicated, may hold values 0 or 1
- template_volume: float32 [64, 64, 64], replicated, may hold values from -6 to 6
- rotation_samples: int32 [64, 4096], P('orient', 'slab'), may hold values from 0 to 262143
Outputs:
- scores: bfloat16 [192, 128, 128], P('slab', 'orient')
Inputs may be any that keep to these rules, and one draw needn't show every extreme that they name: `assigned_worker`: the occupied slots of each slab index come first. Slab indices 2m and 2m+1 hold 24 occupied slots together, and some slab index has all 24 occupied. The occupied slots, taken in slot order over all slab indices, are dealt to the workers in turn, so every worker receives exactly 12 tiles and at most 3 from one slab index.
All inputs are finite; a program needn't handle non-finite values.
Results may differ from a plain program's by a relative error of at most 0.0085.
Values may be sent and summed in bfloat16 or wider, within the bound.
No kernel may reach another device: no remote copies, remote signals or barrier semaphores. Data moves between devices by JAX's collectives and lax.ppermute only.
A program may use at most 128 MiB of HBM per device.

v0:
```python
import math
import jax
import jax.numpy as jnp
from jax import lax
from jax.sharding import PartitionSpec as P


def partner(block, axis, bit):
    count = lax.axis_size(axis)
    route = []
    for low in range(count):
        high = low | 1 << bit
        if high != low and high < count:
            route += [(low, high), (high, low)]
    return lax.ppermute(block, axis, route)


def tables(length):
    counter = jnp.arange(length, dtype=jnp.int32)
    angles = (counter[:, None] * counter[None, :] % length).astype(jnp.float32) * (
        2.0 * math.pi / length
    )
    return (jnp.cos(angles).astype(jnp.bfloat16), jnp.sin(angles).astype(jnp.bfloat16))


def band_table(length, box_edge):
    counter = jnp.arange(length, dtype=jnp.int32)
    offsets = (counter[None, :] - counter[:, None]) % length
    return (offsets < box_edge).astype(jnp.float32)


def right_mul(values, table):
    return jnp.einsum("...ab,bc->...ac", values, table, preferred_element_type=jnp.float32)


def left_mul(table, values):
    return jnp.einsum("ka,...ab->...kb", table, values, preferred_element_type=jnp.float32)


def forward_two(values, cosine_table, sine_table):
    first_real = right_mul(values, cosine_table).astype(jnp.bfloat16)
    first_imag = (-right_mul(values, sine_table)).astype(jnp.bfloat16)
    second_real = (left_mul(cosine_table, first_real) + left_mul(sine_table, first_imag)).astype(
        jnp.bfloat16
    )
    second_imag = (left_mul(cosine_table, first_imag) - left_mul(sine_table, first_real)).astype(
        jnp.bfloat16
    )
    return (second_real, second_imag)


def inverse_real(real_part, imag_part, cosine_table, sine_table):
    length = real_part.shape[-1]
    first_real = (right_mul(real_part, cosine_table) - right_mul(imag_part, sine_table)).astype(
        jnp.bfloat16
    )
    first_imag = (right_mul(imag_part, cosine_table) + right_mul(real_part, sine_table)).astype(
        jnp.bfloat16
    )
    return (left_mul(cosine_table, first_real) - left_mul(sine_table, first_imag)) * (
        1.0 / (length * length)
    )


def filtered(values, wedge_weight, cosine_table, sine_table):
    spec_real, spec_imag = forward_two(values, cosine_table, sine_table)
    return inverse_real(
        spec_real * wedge_weight, spec_imag * wedge_weight, cosine_table, sine_table
    ).astype(jnp.bfloat16)


def pick_rows(chosen, source):
    counter = jnp.arange(source.shape[0], dtype=jnp.int32)
    selector = (chosen[:, None] == counter[None, :]).astype(source.dtype)
    flat = source.reshape(source.shape[0], -1)
    picked = jnp.dot(selector, flat, preferred_element_type=jnp.float32).astype(source.dtype)
    return picked.reshape((chosen.shape[0],) + source.shape[1:])


def make_templates(
    template_volume, rotation_samples, box_edge, planes, tile_len, cosine_table, sine_table
):
    count = rotation_samples.shape[0]
    sampled_part = jnp.take(template_volume.reshape(-1), rotation_samples, axis=0).astype(
        jnp.bfloat16
    )
    sampled = lax.all_gather(sampled_part, "slab", axis=1, tiled=True)
    sampled = sampled.reshape(count, planes, box_edge, box_edge)
    padded = jnp.pad(sampled, ((0, 0), (0, 0), (0, tile_len - box_edge), (0, tile_len - box_edge)))
    template_norm = jnp.sqrt(
        jnp.sum(jnp.square(sampled.astype(jnp.float32)), axis=(1, 2, 3)) + 1e-05
    )
    spec_real, spec_imag = forward_two(padded, cosine_table, sine_table)
    return (spec_real, spec_imag, template_norm)


def score_tiles(
    slab_field, templ_real, templ_imag, template_norm, cosine_table, sine_table, band_sum, box_edge
):
    planes = slab_field.shape[1]
    field_real, field_imag = forward_two(slab_field, cosine_table, sine_table)
    left_real = field_real.astype(jnp.float32)[:, None]
    left_imag = field_imag.astype(jnp.float32)[:, None]
    right_real = templ_real.astype(jnp.float32)[None]
    right_imag = templ_imag.astype(jnp.float32)[None]
    prod_real = jnp.sum(left_real * right_real + left_imag * right_imag, axis=2).astype(
        jnp.bfloat16
    )
    prod_imag = jnp.sum(left_imag * right_real - left_real * right_imag, axis=2).astype(
        jnp.bfloat16
    )
    correlation = inverse_real(prod_real, prod_imag, cosine_table, sine_table)
    energy = jnp.sum(jnp.square(slab_field.astype(jnp.float32)), axis=1)
    summed = jnp.einsum(
        "ka,nab,lb->nkl", band_sum, energy, band_sum, precision=lax.Precision.HIGHEST
    )
    local_rms = jnp.sqrt(summed / (box_edge * box_edge * planes) + 1e-05)
    ratio = correlation / (local_rms[:, None] * template_norm[None, :, None, None])
    return jnp.max(ratio, axis=1)


def orient_max(best):
    groups = lax.axis_size("orient")
    parts = lax.all_to_all(best, "orient", split_axis=1, concat_axis=0, tiled=True)
    stacked = parts.reshape(groups, best.shape[0], parts.shape[1], parts.shape[2])
    return jnp.max(stacked, axis=0)


def per_device(tiles, assigned_worker, wedge_mask, template_volume, rotation_samples):
    tile_len = tiles.shape[-1]
    planes = tiles.shape[1]
    home_slots = tiles.shape[0]
    work_slots = home_slots // 2
    box_edge = template_volume.shape[0]
    cosine_table, sine_table = tables(tile_len)
    band_sum = band_table(tile_len, box_edge)
    wedge_weight = wedge_mask.astype(jnp.bfloat16)
    templ_real, templ_imag, template_norm = make_templates(
        template_volume, rotation_samples, box_edge, planes, tile_len, cosine_table, sine_table
    )
    occupied = assigned_worker >= 0
    own_count = jnp.sum(occupied.astype(jnp.int32))
    partner_tiles = partner(tiles[work_slots:], "slab", 0)
    counter = jnp.arange(work_slots, dtype=jnp.int32)
    keep_own = (counter < own_count)[:, None, None, None]
    moved_in = pick_rows(counter - own_count, partner_tiles)
    gathered = jnp.where(keep_own, tiles[:work_slots], moved_in)
    slab_field = filtered(gathered, wedge_weight, cosine_table, sine_table)
    best = score_tiles(
        slab_field,
        templ_real,
        templ_imag,
        template_norm,
        cosine_table,
        sine_table,
        band_sum,
        box_edge,
    )
    best_rows = orient_max(best.astype(jnp.bfloat16))
    outgoing = pick_rows(counter + own_count, best_rows)
    returned = partner(outgoing, "slab", 0)
    result = jnp.concatenate([best_rows, returned], axis=0)
    return jnp.where(occupied[:, None, None], result, jnp.zeros_like(result))


def solution(mesh):
    return jax.shard_map(
        per_device,
        mesh=mesh,
        in_specs=(P("slab", None, None, None), P("slab"), P(), P(), P("orient", "slab")),
        out_specs=P("slab", "orient", None),
        check_vma=False,
    )
```

profile of v0, /device:TPU:0, one launch (start us, length us, event | category | flops | bytes accessed | tf_op | source)
XLA Modules:
  0.0 180.5 jit_solution(15834255213761315557)
XLA Ops:
  0.0 1.8 slice.7
  1.8 2.9 %collective-permute-start = (bf16[12,1,128,128]{3,2,1,0:T(8,128)(2,1)}, bf16[12,1,128,128]{3,2,1,0:T(8,128)(2,1)}, u32[]{:S(2)}, u32[]{:S(2)}) collective-permute-start(bf16[12,1,128,128]{3,2,1,0:T(8,128)(2,1)} %slice.7), channel_id=1, source_target_pairs={{0,4},{4,0},{8,12},{12,8},{16,20},{20,16},{24,28},{28,24},{1,5},{5... | collective-permute-start | bytes 1179656 | tf_op jit(solution)/shard_map/ppermute | solution.py:15
  4.7 1.9 %reshape.192 = bf16[262144]{0:T(1024)(128)(2,1)S(1)} reshape(f32[64,64,64]{2,1,0:T(8,128)} %param.8) | data formatting | bytes 1572864 | tf_op jit(solution)/shard_map/reshape | solution.py:84
  6.6 0.8 fusion.131
  7.4 0.0 copy-start.2
  7.4 50.7 %gather_fusion = bf16[8192]{0:T(1024)(128)(2,1)S(1)} fusion(bf16[262144]{0:T(1024)(128)(2,1)S(1)} %reshape.192, s32[8192]{0:T(1024)S(1)} %broadcast_clamp_fusion), kind=kCustom, calls=%fused_computation | custom fusion | bytes 65536 | tf_op jit(solution)/shard_map/jit(_take)/gather | solution.py:84
  58.1 0.0 copy-done.1
  58.2 30.9 %all_gather.3 = bf16[16,4096]{1,0:T(8,128)(2,1)S(1)} all-gather(bf16[16,512]{1,0:T(8,128)(2,1)S(1)} %select_convert_fusion), channel_id=1, replica_groups=mesh['slab'=8,'orient'=4] {'slab'}, dimensions={1}, use_global_device_ids=true | all-gather | bytes 147456 | tf_op jit(solution)/shard_map/all_gather | solution.py:87
  89.0 0.2 reshape.193
  89.3 0.5 fusion.25
  89.8 0.5 convolution_convert_fusion.2
  90.3 0.5 fusion.103
  90.9 0.5 fusion.107
  91.4 0.5 fusion.40
  92.0 0.0 copy-done.3
  92.0 0.6 convert_reduce_fusion
  92.6 0.6 iota_add_fusion
  93.3 0.5 fusion.43
  93.8 0.7 iota_compare_fusion.4
  94.5 0.3 copy.137
  94.8 0.0 copy-done.2
  94.8 0.1 copy.115
  95.0 0.3 copy.131
  95.3 0.1 multiply_reduce_fusion
  95.5 0.0 collective-permute-done
  95.5 1.0 pad.8
  96.5 0.3 copy.171
  96.9 0.3 convolution_convert_fusion
  97.2 0.1 copy.172
  97.3 1.5 convolution_convert_fusion.4
  98.8 1.5 fusion.29
  100.3 0.5 fusion.120
  100.8 0.5 fusion.116
  101.3 0.5 fusion.54
  101.9 1.4 fusion.118
  103.2 0.5 fusion.56
  103.8 1.4 fusion.113
  105.1 2.9 %fusion.50 = f32[12,128,128]{2,1,0:T(8,128)} fusion(f32[12,128,128]{2,1,0:T(8,128)} %fusion.118, bf16[12,128,128]{1,2,0:T(8,128)(2,1)S(1)} %fusion.56), kind=kOutput, calls=%fused_computation.74 | convolution fusion | flops 101548032 | bytes 1966080 | tf_op jit(solution)/shard_map/ka,...ab->...kb/dot_general | solution.py:37
  108.0 2.2 %fusion.34 = bf16[12,128,128]{2,1,0:T(8,128)(2,1)S(1)} fusion(f32[12,128,128]{2,1,0:T(8,128)} %fusion.50, f32[12,128,128]{2,1,0:T(8,128)} %fusion.113, bf16[12,128,128]{1,2,0:T(8,128)(2,1)S(1)} %fusion.54), kind=kOutput, calls=%fused_computation.56 | convolution fusion | flops 102137856 | bytes 2359296 | tf_op jit(solution)/shard_map/ka,...ab->...kb/dot_general | solution.py:37
  110.2 0.5 fusion.35
  110.7 0.5 convolution_convert_fusion.3
  111.2 1.5 fusion.57
  112.7 0.5 fusion.105
  113.2 1.4 fusion.110
  114.6 1.4 fusion.46
  116.0 1.4 copy.134
  117.4 2.5 %fusion.49 = f32[12,128,128]{1,2,0:T(8,128)} fusion(f32[12,128,128]{2,1,0:T(8,128)} %fusion.110, bf16[12,128,128]{2,1,0:T(8,128)(2,1)S(1)} %fusion.35), kind=kOutput, calls=%fused_computation.73 | convolution fusion | flops 51167232 | bytes 1966080 | tf_op jit(solution)/shard_map/ka,...ab->...kb/dot_general | solution.py:37
  119.9 2.3 %copy.128 = f32[12,128,128]{2,1,0:T(8,128)} copy(f32[12,128,128]{1,2,0:T(8,128)} %fusion.49) | data formatting | bytes 1572864 | tf_op jit(solution)/shard_map/mul | solution.py:106
  122.2 6.9 %fusion.2 = f32[12,16,128,128]{3,2,1,0:T(8,128)} fusion(f32[16,128,128]{2,1,0:T(8,128)S(1)} %copy.137, f32[12,128,128]{2,1,0:T(8,128)S(1)} %copy.134, f32[16,128,128]{2,1,0:T(8,128)S(1)} %copy.131, f32[12,128,128]{2,1,0:T(8,128)} %copy.128), kind=kOutput, calls=%fused_computation.9 | convolution fusion | flops 818135040 | bytes 16252928 | tf_op jit(solution)/shard_map/...ab,bc->...ac/dot_general | solution.py:33
  129.1 0.0 copy-done
  129.1 5.8 %fusion.1 = f32[12,16,128,128]{3,2,1,0:T(8,128)} fusion(f32[16,128,128]{2,1,0:T(8,128)S(1)} %copy.137, f32[12,128,128]{2,1,0:T(8,128)S(1)} %copy.134, f32[16,128,128]{2,1,0:T(8,128)S(1)} %copy.131, f32[12,128,128]{2,1,0:T(8,128)S(1)} %copy-done), kind=kOutput, calls=%fused_computation.8 | convolution fusion | flops 818135040 | bytes 16252928 | tf_op jit(solution)/shard_map/...ab,bc->...ac/dot_general | solution.py:33
  134.9 10.1 %fusion.5 = f32[12,16,128,128]{3,2,1,0:T(8,128)} fusion(f32[12,16,128,128]{3,2,1,0:T(8,128)} %fusion.2, f32[16,128,128]{2,1,0:T(8,128)S(1)} %copy.137, f32[12,128,128]{2,1,0:T(8,128)S(1)} %copy.134, f32[16,128,128]{2,1,0:T(8,128)S(1)} %copy.131, f32[12,128,128]{2,1,0:T(8,128)} %copy.128), kind=kOutput, calls=%fused_computation.12 | convolution fusion | flops 1629978624 | bytes 28835840 | tf_op jit(solution)/shard_map/ka,...ab->...kb/dot_general | solution.py:37
  144.9 2.7 %fusion.27 = f32[12,128,128]{2,1,0:T(8,128)} fusion(f32[12,128,128]{1,2,0:T(8,128)} %fusion.57), kind=kOutput, calls=%fused_computation.40 | convolution fusion | flops 302596096 | bytes 1572864 | tf_op jit(solution)/shard_map/ka,nab,lb->nkl/dot_general | solution.py:114
  147.6 2.3 %copy.141 = f32[12,128,128]{1,2,0:T(8,128)} copy(f32[12,128,128]{2,1,0:T(8,128)} %fusion.27) | data formatting | bytes 1572864 | tf_op jit(solution)/shard_map/sqrt | solution.py:117
  150.0 12.2 %fusion = bf16[12,128,128]{1,2,0:T(8,128)(2,1)S(1)} fusion(f32[12,16,128,128]{3,2,1,0:T(8,128)} %fusion.5, f32[16]{0:T(128)S(1)} %add_sqrt_fusion, f32[12,128,128]{1,2,0:T(8,128)} %copy.141, f32[12,16,128,128]{3,2,1,0:T(8,128)} %fusion.1, f32[16,128,128]{2,1,0:T(8,128)S(1)} %copy.137, f32[12,128,128]{2,1,0:T(8,128)S(1)} %copy.134, ...), kind=kOutput, calls=%fused_computation.7 | convolution fusion | flops 1645510656 | bytes 30015552 | tf_op jit(solution)/shard_map/ka,...ab->...kb/dot_general | solution.py:37
  162.2 0.4 copy.142
  162.6 11.5 %all_to_all.12 = bf16[12,128,128]{2,0,1:T(8,128)(2,1)S(1)} all-to-all(bf16[12,128,128]{2,0,1:T(8,128)(2,1)S(1)} %copy.142), channel_id=1, replica_groups=mesh['slab'=8,'orient'=4] {'orient'}, dimensions={1} | all-to-all | bytes 786432 | tf_op jit(solution)/shard_map/all_to_all | solution.py:124
  174.1 0.1 reduce_max.19
  174.2 0.1 copy.174
  174.3 0.2 convolution_convert_fusion.1
  174.6 0.6 collective-permute-start.1
  175.2 4.4 %collective-permute-done.1 = bf16[12,32,128]{2,0,1:T(8,128)(2,1)S(1)} collective-permute-done((bf16[12,32,128]{2,0,1:T(8,128)(2,1)S(1)}, bf16[12,32,128]{2,0,1:T(8,128)(2,1)S(1)}, u32[]{:S(2)}, u32[]{:S(2)}) %collective-permute-start.1) | collective-permute-done | bytes 98336 | tf_op jit(solution)/shard_map/ppermute | solution.py:15
  179.7 0.1 maximum_select_fusion
  179.8 0.7 copy.145
  (15 shorter events, 0.2 us)
Async XLA Ops:
  0.0 58.1 %copy-start.1 = (s32[16,512]{1,0:T(8,128)S(1)}, s32[16,512]{1,0:T(8,128)}, u32[]{:S(2)}) copy-start(s32[16,512]{1,0:T(8,128)} %param.9) | copy-start | bytes 98308
  1.8 93.7 %collective-permute-start = (bf16[12,1,128,128]{3,2,1,0:T(8,128)(2,1)}, bf16[12,1,128,128]{3,2,1,0:T(8,128)(2,1)}, u32[]{:S(2)}, u32[]{:S(2)}) collective-permute-start(bf16[12,1,128,128]{3,2,1,0:T(8,128)(2,1)} %slice.7), channel_id=1, source_target_pairs={{0,4},{4,0},{8,12},{12,8},{16,20},{20,16},{24,28},{28,24},{1,5},{5... | collective-permute-start | bytes 1179656 | tf_op jit(solution)/shard_map/ppermute | solution.py:15
  7.3 84.6 %copy-start.3 = (s32[24]{0:T(128)S(1)}, s32[24]{0:T(128)}, u32[]{:S(2)}) copy-start(s32[24]{0:T(128)} %param.6) | copy-start | bytes 292
  7.4 87.4 %copy-start.2 = (s32[128,128]{1,0:T(8,128)S(1)}, s32[128,128]{1,0:T(8,128)}, u32[]{:S(2)}) copy-start(s32[128,128]{1,0:T(8,128)} %param.7) | copy-start | bytes 196612
  122.2 6.9 %copy-start = (f32[12,128,128]{2,1,0:T(8,128)S(1)}, f32[12,128,128]{2,1,0:T(8,128)}, u32[]{:S(2)}) copy-start(f32[12,128,128]{2,1,0:T(8,128)} %copy.128) | copy-start | bytes 2359300
  174.6 5.0 %collective-permute-start.1 = (bf16[12,32,128]{2,0,1:T(8,128)(2,1)S(1)}, bf16[12,32,128]{2,0,1:T(8,128)(2,1)S(1)}, u32[]{:S(2)}, u32[]{:S(2)}) collective-permute-start(bf16[12,32,128]{2,0,1:T(8,128)(2,1)S(1)} %copy.144), channel_id=1, source_target_pairs={{0,4},{4,0},{8,12},{12,8},{16,20},{20,16},{24,28},{28,24},{1,5},{5... | collective-permute-start | bytes 294920 | tf_op jit(solution)/shard_map/ppermute | solution.py:15
where the time goes:
time: 181 us; the launch traced here: 180 us
  local copies, waits for them, and re-layouts  64.2 us (35%)
  matrix products  62.5 us (35%)
  blocking collectives  42.3 us (23%)
  waiting for transfers between devices  4.44 us (2%)
  starting transfers between devices  3.53 us (2%)
  other arithmetic  3.09 us (2%)
    gather x2, local copies, waits for them, and re-layouts, make_templates(): jnp.take(template_volume.reshape(-1), rotation_samples, axis=0)  50.7 us
    dot_general x16, matrix products, left_mul(): jnp.einsum('ka,...ab->...kb', table, values, preferred_element_type=jnp.f...  37.3 us
    all_gather x1, blocking collectives, make_templates(): sampled = lax.all_gather(sampled_part, 'slab', axis=1, tiled=True)  30.9 us
    dot_general x10, matrix products, right_mul(): jnp.einsum('...ab,bc->...ac', values, table, preferred_element_type=jnp.f...  20.4 us
    all_to_all x1, blocking collectives, orient_max(): lax.all_to_all(best, 'orient', split_axis=1, concat_axis=0, tiled=True)  11.5 us
    ppermute x2, waiting for transfers between devices, partner(): return lax.ppermute(block, axis, route)  4.44 us
    dot_general x2, matrix products, score_tiles(): jnp.einsum('ka,nab,lb->nkl', band_sum, energy, band_sum, precision=lax.Pr...  4.21 us
  transfers between devices with their start and end apart: 2, of which 1 were waited for; matrix products, arithmetic and copies ran while one was open for 33% of the time, Pallas kernels for 0%

commit v1 on v0

--- a/solution.py
+++ b/solution.py
@@ -3,6 +3,16 @@
 import jax.numpy as jnp
 from jax import lax
 from jax.sharding import PartitionSpec as P
+
+
+def gather_by_hops(x, name, along):
+    peers = lax.axis_size(name)
+    held, blocks = (x, [x])
+    for _ in range(peers - 1):
+        held = lax.ppermute(held, name, [(i, (i + 1) % peers) for i in range(peers)])
+        blocks.insert(0, held)
+    line = jnp.concatenate(blocks, axis=along)
+    return jnp.roll(line, (lax.axis_index(name) + 1) * x.shape[along], axis=along)
 
 
 def partner(block, axis, bit):
@@ -84,7 +94,7 @@
     sampled_part = jnp.take(template_volume.reshape(-1), rotation_samples, axis=0).astype(
         jnp.bfloat16
     )
-    sampled = lax.all_gather(sampled_part, "slab", axis=1, tiled=True)
+    sampled = gather_by_hops(sampled_part, "slab", 1)
     sampled = sampled.reshape(count, planes, box_edge, box_edge)
     padded = jnp.pad(sampled, ((0, 0), (0, 0), (0, tile_len - box_edge), (0, tile_len - box_edge)))
     template_norm = jnp.sqrt(

time: 181 us -> 193 us (1.066)
  waiting for transfers between devices: 4.44 us -> 44.5 us
  blocking collectives: 42.3 us -> 11.5 us
  matrix products: 62.5 us -> 65.4 us
    ppermute x0 -> x7, waiting for transfers between devices: none -> 39.5 us  [gather_by_hops(): lax.ppermute(held, name, [(i, (i + 1) % peers) for i in range(peers)])]
    all_gather x1 -> x0, blocking collectives: 30.9 us -> none  [make_templates(): sampled = lax.all_gather(sampled_part, 'slab', axis=1, tiled=True)]
    ppermute x2, starting transfers between devices: 3.53 us -> 0.07 us  [partner(): return lax.ppermute(block, axis, route)]
    ppermute x0 -> x7, starting transfers between devices: none -> 3.02 us  [gather_by_hops(): lax.ppermute(held, name, [(i, (i + 1) % peers) for i in range(peers)])]
    dot_general x16, matrix products: 37.3 us -> 39.8 us  [left_mul(): jnp.einsum('ka,...ab->...kb', table, values, preferred_element_type=jnp.f...]
  transfers between devices with their start and end apart: 2 -> 9, of which waited for: 1 -> 8; matrix products, arithmetic and copies ran while one was open for 33% -> 5% of each run, Pallas kernels for 0% -> 0%
where the time goes in v1:
time: 193 us; the launch traced here: 192 us
  matrix products  65.4 us (34%)
  local copies, waits for them, and re-layouts  63.2 us (33%)
  waiting for transfers between devices  44.5 us (23%)
  blocking collectives  11.5 us (6%)
  other arithmetic  4.21 us (2%)
  starting transfers between devices  3.09 us (2%)
    gather x2, local copies, waits for them, and re-layouts, make_templates(): jnp.take(template_volume.reshape(-1), rotation_samples, axis=0)  50.7 us
    dot_general x16, matrix products, left_mul(): jnp.einsum('ka,...ab->...kb', table, values, preferred_element_type=jnp.f...  39.8 us
    ppermute x7, waiting for transfers between devices, gather_by_hops(): lax.ppermute(held, name, [(i, (i + 1) % peers) for i in range(peers)])  39.5 us
    dot_general x10, matrix products, right_mul(): jnp.einsum('...ab,bc->...ac', values, table, preferred_element_type=jnp.f...  20.8 us
    all_to_all x1, blocking collectives, orient_max(): lax.all_to_all(best, 'orient', split_axis=1, concat_axis=0, tiled=True)  11.5 us
    ppermute x2, waiting for transfers between devices, partner(): return lax.ppermute(block, axis, route)  4.94 us
    dot_general x2, matrix products, score_tiles(): jnp.einsum('ka,nab,lb->nkl', band_sum, energy, band_sum, precision=lax.Pr...  4.18 us
  transfers between devices with their start and end apart: 9, of which 8 were waited for; matrix products, arithmetic and copies ran while one was open for 5% of the time, Pallas kernels for 0%

profile of v1, /device:TPU:0, one launch (start us, length us, event | category | flops | bytes accessed | tf_op | source)
XLA Modules:
  0.0 192.3 jit_solution(4574218473737472239)
XLA Ops:
  0.0 1.9 %reshape.192 = bf16[262144]{0:T(1024)(128)(2,1)S(1)} reshape(f32[64,64,64]{2,1,0:T(8,128)} %param.8) | data formatting | bytes 1572864 | tf_op jit(solution)/shard_map/reshape | solution.py:94
  2.0 0.8 fusion.131
  2.8 50.7 %gather_fusion = bf16[8192]{0:T(1024)(128)(2,1)S(1)} fusion(bf16[262144]{0:T(1024)(128)(2,1)S(1)} %reshape.192, s32[8192]{0:T(1024)S(1)} %broadcast_clamp_fusion), kind=kCustom, calls=%fused_computation | custom fusion | bytes 65536 | tf_op jit(solution)/shard_map/jit(_take)/gather | solution.py:94
  53.5 3.0 %collective-permute-start.1 = (bf16[16,512]{1,0:T(8,128)(2,1)S(1)}, bf16[16,512]{1,0:T(8,128)(2,1)S(1)}, u32[]{:S(2)}, u32[]{:S(2)}) collective-permute-start(bf16[16,512]{1,0:T(8,128)(2,1)S(1)} %select_convert_fusion), channel_id=1, source_target_pairs={{0,4},{4,8},{8,12},{12,16},{16,20},{20,24},{24,28},{28,0},{1,5},{5... | collective-permute-start | bytes 49160 | tf_op jit(solution)/shard_map/ppermute | solution.py:12
  56.6 4.8 %collective-permute-done.1 = bf16[16,512]{1,0:T(8,128)(2,1)S(1)} collective-permute-done((bf16[16,512]{1,0:T(8,128)(2,1)S(1)}, bf16[16,512]{1,0:T(8,128)(2,1)S(1)}, u32[]{:S(2)}, u32[]{:S(2)}) %collective-permute-start.1) | collective-permute-done | bytes 16416 | tf_op jit(solution)/shard_map/ppermute | solution.py:12
  61.3 6.4 %collective-permute-done.2 = bf16[16,512]{1,0:T(8,128)(2,1)S(1)} collective-permute-done((bf16[16,512]{1,0:T(8,128)(2,1)S(1)}, bf16[16,512]{1,0:T(8,128)(2,1)S(1)}, u32[]{:S(2)}, u32[]{:S(2)}) %collective-permute-start.2) | collective-permute-done | bytes 16416 | tf_op jit(solution)/shard_map/ppermute | solution.py:12
  67.7 6.4 %collective-permute-done.3 = bf16[16,512]{1,0:T(8,128)(2,1)S(1)} collective-permute-done((bf16[16,512]{1,0:T(8,128)(2,1)S(1)}, bf16[16,512]{1,0:T(8,128)(2,1)S(1)}, u32[]{:S(2)}, u32[]{:S(2)}) %collective-permute-start.3) | collective-permute-done | bytes 16416 | tf_op jit(solution)/shard_map/ppermute | solution.py:12
  74.2 0.8 slice.7
  75.0 5.7 %collective-permute-done.4 = bf16[16,512]{1,0:T(8,128)(2,1)S(1)} collective-permute-done((bf16[16,512]{1,0:T(8,128)(2,1)S(1)}, bf16[16,512]{1,0:T(8,128)(2,1)S(1)}, u32[]{:S(2)}, u32[]{:S(2)}) %collective-permute-start.4) | collective-permute-done | bytes 16416 | tf_op jit(solution)/shard_map/ppermute | solution.py:12
  80.7 0.6 convert_reduce_fusion
  81.4 5.9 %collective-permute-done.5 = bf16[16,512]{1,0:T(8,128)(2,1)S(1)} collective-permute-done((bf16[16,512]{1,0:T(8,128)(2,1)S(1)}, bf16[16,512]{1,0:T(8,128)(2,1)S(1)}, u32[]{:S(2)}, u32[]{:S(2)}) %collective-permute-start.5) | collective-permute-done | bytes 16416 | tf_op jit(solution)/shard_map/ppermute | solution.py:12
  87.3 0.6 iota_add_fusion
  87.9 5.8 %collective-permute-done.6 = bf16[16,512]{1,0:T(8,128)(2,1)S(1)} collective-permute-done((bf16[16,512]{1,0:T(8,128)(2,1)S(1)}, bf16[16,512]{1,0:T(8,128)(2,1)S(1)}, u32[]{:S(2)}, u32[]{:S(2)}) %collective-permute-start.6) | collective-permute-done | bytes 16416 | tf_op jit(solution)/shard_map/ppermute | solution.py:12
  93.7 1.2 iota_compare_fusion.4
  95.0 0.7 copy.115
  95.7 4.5 %collective-permute-done.7 = bf16[16,512]{1,0:T(8,128)(2,1)S(1)} collective-permute-done((bf16[16,512]{1,0:T(8,128)(2,1)S(1)}, bf16[16,512]{1,0:T(8,128)(2,1)S(1)}, u32[]{:S(2)}, u32[]{:S(2)}) %collective-permute-start.7) | collective-permute-done | bytes 16416 | tf_op jit(solution)/shard_map/ppermute | solution.py:12
  100.3 0.2 multiply_reduce_fusion
  100.5 0.2 reshape.193
  100.7 0.5 fusion.25
  101.3 0.5 convolution_convert_fusion.2
  101.8 0.5 fusion.103
  102.3 0.5 fusion.107
  102.9 0.5 fusion.40
  103.4 0.3 copy.137
  103.8 1.6 fusion.43
  105.4 0.3 copy.131
  105.7 0.5 add_sqrt_fusion
  106.3 0.3 copy.171
  106.6 0.3 convolution_convert_fusion
  107.0 0.1 copy.172
  107.1 1.5 convolution_convert_fusion.4
  108.6 1.5 fusion.29
  110.1 0.5 fusion.120
  110.6 0.5 fusion.116
  111.1 1.3 fusion.54
  112.4 1.4 fusion.118
  113.8 1.3 fusion.56
  115.0 1.4 fusion.113
  116.4 2.8 %fusion.50 = f32[12,128,128]{2,1,0:T(8,128)} fusion(f32[12,128,128]{2,1,0:T(8,128)} %fusion.118, bf16[12,128,128]{1,2,0:T(8,128)(2,1)S(1)} %fusion.56), kind=kOutput, calls=%fused_computation.74 | convolution fusion | flops 101548032 | bytes 1966080 | tf_op jit(solution)/shard_map/ka,...ab->...kb/dot_general | solution.py:47
  119.3 2.2 %fusion.34 = bf16[12,128,128]{2,1,0:T(8,128)(2,1)S(1)} fusion(f32[12,128,128]{2,1,0:T(8,128)} %fusion.50, f32[12,128,128]{2,1,0:T(8,128)} %fusion.113, bf16[12,128,128]{1,2,0:T(8,128)(2,1)S(1)} %fusion.54), kind=kOutput, calls=%fused_computation.56 | convolution fusion | flops 102137856 | bytes 2359296 | tf_op jit(solution)/shard_map/ka,...ab->...kb/dot_general | solution.py:47
  121.4 0.5 fusion.35
  122.0 0.5 convolution_convert_fusion.3
  122.5 1.5 fusion.57
  124.0 0.5 fusion.105
  124.5 1.4 fusion.110
  125.9 1.4 fusion.46
  127.3 1.6 copy.134
  128.8 2.5 %fusion.49 = f32[12,128,128]{1,2,0:T(8,128)} fusion(f32[12,128,128]{2,1,0:T(8,128)} %fusion.110, bf16[12,128,128]{2,1,0:T(8,128)(2,1)S(1)} %fusion.35), kind=kOutput, calls=%fused_computation.73 | convolution fusion | flops 51167232 | bytes 1966080 | tf_op jit(solution)/shard_map/ka,...ab->...kb/dot_general | solution.py:47
  131.4 2.3 %copy.128 = f32[12,128,128]{2,1,0:T(8,128)} copy(f32[12,128,128]{1,2,0:T(8,128)} %fusion.49) | data formatting | bytes 1572864 | tf_op jit(solution)/shard_map/mul | solution.py:116
  133.7 7.1 %fusion.2 = f32[12,16,128,128]{3,2,1,0:T(8,128)} fusion(f32[16,128,128]{2,1,0:T(8,128)S(1)} %copy.137, f32[12,128,128]{2,1,0:T(8,128)S(1)} %copy.134, f32[16,128,128]{2,1,0:T(8,128)S(1)} %copy.131, f32[12,128,128]{2,1,0:T(8,128)} %copy.128), kind=kOutput, calls=%fused_computation.9 | convolution fusion | flops 818135040 | bytes 16252928 | tf_op jit(solution)/shard_map/...ab,bc->...ac/dot_general | solution.py:43
  140.8 5.9 %fusion.1 = f32[12,16,128,128]{3,2,1,0:T(8,128)} fusion(f32[16,128,128]{2,1,0:T(8,128)S(1)} %copy.137, f32[12,128,128]{2,1,0:T(8,128)S(1)} %copy.134, f32[16,128,128]{2,1,0:T(8,128)S(1)} %copy.131, f32[12,128,128]{2,1,0:T(8,128)S(1)} %copy-done), kind=kOutput, calls=%fused_computation.8 | convolution fusion | flops 818135040 | bytes 16252928 | tf_op jit(solution)/shard_map/...ab,bc->...ac/dot_general | solution.py:43
  146.6 10.1 %fusion.5 = f32[12,16,128,128]{3,2,1,0:T(8,128)} fusion(f32[12,16,128,128]{3,2,1,0:T(8,128)} %fusion.2, f32[16,128,128]{2,1,0:T(8,128)S(1)} %copy.137, f32[12,128,128]{2,1,0:T(8,128)S(1)} %copy.134, f32[16,128,128]{2,1,0:T(8,128)S(1)} %copy.131, f32[12,128,128]{2,1,0:T(8,128)} %copy.128), kind=kOutput, calls=%fused_computation.12 | convolution fusion | flops 1629978624 | bytes 28835840 | tf_op jit(solution)/shard_map/ka,...ab->...kb/dot_general | solution.py:47
  156.7 2.7 %fusion.27 = f32[12,128,128]{2,1,0:T(8,128)} fusion(f32[12,128,128]{1,2,0:T(8,128)} %fusion.57), kind=kOutput, calls=%fused_computation.40 | convolution fusion | flops 302596096 | bytes 1572864 | tf_op jit(solution)/shard_map/ka,nab,lb->nkl/dot_general | solution.py:124
  159.4 2.3 %copy.141 = f32[12,128,128]{1,2,0:T(8,128)} copy(f32[12,128,128]{2,1,0:T(8,128)} %fusion.27) | data formatting | bytes 1572864 | tf_op jit(solution)/shard_map/sqrt | solution.py:127
  161.7 12.2 %fusion = bf16[12,128,128]{1,2,0:T(8,128)(2,1)S(1)} fusion(f32[12,16,128,128]{3,2,1,0:T(8,128)} %fusion.5, f32[16]{0:T(128)S(1)} %copy-done.6, f32[12,128,128]{1,2,0:T(8,128)} %copy.141, f32[12,16,128,128]{3,2,1,0:T(8,128)} %fusion.1, f32[16,128,128]{2,1,0:T(8,128)S(1)} %copy.137, f32[12,128,128]{2,1,0:T(8,128)S(1)} %copy.134, ...), kind=kOutput, calls=%fused_computation.7 | convolution fusion | flops 1645510656 | bytes 30015552 | tf_op jit(solution)/shard_map/ka,...ab->...kb/dot_general | solution.py:47
  173.9 0.4 copy.142
  174.4 11.5 %all_to_all.12 = bf16[12,128,128]{2,0,1:T(8,128)(2,1)S(1)} all-to-all(bf16[12,128,128]{2,0,1:T(8,128)(2,1)S(1)} %copy.142), channel_id=1, replica_groups=mesh['slab'=8,'orient'=4] {'orient'}, dimensions={1} | all-to-all | bytes 786432 | tf_op jit(solution)/shard_map/all_to_all | solution.py:134
  185.9 0.1 reduce_max.19
  186.0 0.1 copy.174
  186.1 0.2 convolution_convert_fusion.1
  186.4 0.1 collective-permute-start.8
  186.5 4.9 %collective-permute-done.8 = bf16[12,32,128]{2,0,1:T(8,128)(2,1)S(1)} collective-permute-done((bf16[12,32,128]{2,0,1:T(8,128)(2,1)S(1)}, bf16[12,32,128]{2,0,1:T(8,128)(2,1)S(1)}, u32[]{:S(2)}, u32[]{:S(2)}) %collective-permute-start.8) | collective-permute-done | bytes 98336 | tf_op jit(solution)/shard_map/ppermute | solution.py:25
  191.5 0.1 maximum_select_fusion
  191.6 0.7 copy.145
  (50 shorter events, 0.3 us)
Async XLA Ops:
  0.0 53.5 %copy-start.3 = (s32[16,512]{1,0:T(8,128)S(1)}, s32[16,512]{1,0:T(8,128)}, u32[]{:S(2)}) copy-start(s32[16,512]{1,0:T(8,128)} %param.9) | copy-start | bytes 98308
  0.0 74.2 %copy-start.2 = (bf16[24,1,128,128]{3,2,1,0:T(8,128)(2,1)S(1)}, bf16[24,1,128,128]{3,2,1,0:T(8,128)(2,1)}, u32[]{:S(2)}) copy-start(bf16[24,1,128,128]{3,2,1,0:T(8,128)(2,1)} %param.5) | copy-start | bytes 2359300
  0.0 80.7 %copy-start.5 = (s32[24]{0:T(128)S(1)}, s32[24]{0:T(128)}, u32[]{:S(2)}) copy-start(s32[24]{0:T(128)} %param.6) | copy-start | bytes 292
  0.0 95.0 %copy-start.4 = (s32[128,128]{1,0:T(8,128)S(1)}, s32[128,128]{1,0:T(8,128)}, u32[]{:S(2)}) copy-start(s32[128,128]{1,0:T(8,128)} %param.7) | copy-start | bytes 196612
  53.5 7.8 %collective-permute-start.1 = (bf16[16,512]{1,0:T(8,128)(2,1)S(1)}, bf16[16,512]{1,0:T(8,128)(2,1)S(1)}, u32[]{:S(2)}, u32[]{:S(2)}) collective-permute-start(bf16[16,512]{1,0:T(8,128)(2,1)S(1)} %select_convert_fusion), channel_id=1, source_target_pairs={{0,4},{4,8},{8,12},{12,16},{16,20},{20,24},{24,28},{28,0},{1,5},{5... | collective-permute-start | bytes 49160 | tf_op jit(solution)/shard_map/ppermute | solution.py:12
  61.3 6.4 %collective-permute-start.2 = (bf16[16,512]{1,0:T(8,128)(2,1)S(1)}, bf16[16,512]{1,0:T(8,128)(2,1)S(1)}, u32[]{:S(2)}, u32[]{:S(2)}) collective-permute-start(bf16[16,512]{1,0:T(8,128)(2,1)S(1)} %collective-permute-done.1), channel_id=1, source_target_pairs={{0,4},{4,8},{8,12},{12,16},{16,20},{20,24},{24,28},{28,0},{1,5},{5... | collective-permute-start | bytes 49160 | tf_op jit(solution)/shard_map/ppermute | solution.py:12
  67.7 6.4 %collective-permute-start.3 = (bf16[16,512]{1,0:T(8,128)(2,1)S(1)}, bf16[16,512]{1,0:T(8,128)(2,1)S(1)}, u32[]{:S(2)}, u32[]{:S(2)}) collective-permute-start(bf16[16,512]{1,0:T(8,128)(2,1)S(1)} %collective-permute-done.2), channel_id=1, source_target_pairs={{0,4},{4,8},{8,12},{12,16},{16,20},{20,24},{24,28},{28,0},{1,5},{5... | collective-permute-start | bytes 49160 | tf_op jit(solution)/shard_map/ppermute | solution.py:12
  74.2 6.5 %collective-permute-start.4 = (bf16[16,512]{1,0:T(8,128)(2,1)S(1)}, bf16[16,512]{1,0:T(8,128)(2,1)S(1)}, u32[]{:S(2)}, u32[]{:S(2)}) collective-permute-start(bf16[16,512]{1,0:T(8,128)(2,1)S(1)} %collective-permute-done.3), channel_id=1, source_target_pairs={{0,4},{4,8},{8,12},{12,16},{16,20},{20,24},{24,28},{28,0},{1,5},{5... | collective-permute-start | bytes 49160 | tf_op jit(solution)/shard_map/ppermute | solution.py:12
  75.0 31.2 %collective-permute-start = (bf16[12,1,128,128]{3,2,1,0:T(8,128)(2,1)}, bf16[12,1,128,128]{3,2,1,0:T(8,128)(2,1)S(1)}, u32[]{:S(2)}, u32[]{:S(2)}) collective-permute-start(bf16[12,1,128,128]{3,2,1,0:T(8,128)(2,1)} %slice.7), channel_id=1, source_target_pairs={{0,4},{4,0},{8,12},{12,8},{16,20},{20,16},{24,28},{28,24},{1,5},{5... | collective-permute-start | bytes 1179656 | tf_op jit(solution)/shard_map/ppermute | solution.py:25
  80.7 6.6 %collective-permute-start.5 = (bf16[16,512]{1,0:T(8,128)(2,1)S(1)}, bf16[16,512]{1,0:T(8,128)(2,1)S(1)}, u32[]{:S(2)}, u32[]{:S(2)}) collective-permute-start(bf16[16,512]{1,0:T(8,128)(2,1)S(1)} %collective-permute-done.4), channel_id=1, source_target_pairs={{0,4},{4,8},{8,12},{12,16},{16,20},{20,24},{24,28},{28,0},{1,5},{5... | collective-permute-start | bytes 49160 | tf_op jit(solution)/shard_map/ppermute | solution.py:12
  87.3 6.4 %collective-permute-start.6 = (bf16[16,512]{1,0:T(8,128)(2,1)S(1)}, bf16[16,512]{1,0:T(8,128)(2,1)S(1)}, u32[]{:S(2)}, u32[]{:S(2)}) collective-permute-start(bf16[16,512]{1,0:T(8,128)(2,1)S(1)} %collective-permute-done.5), channel_id=1, source_target_pairs={{0,4},{4,8},{8,12},{12,16},{16,20},{20,24},{24,28},{28,0},{1,5},{5... | collective-permute-start | bytes 49160 | tf_op jit(solution)/shard_map/ppermute | solution.py:12
  93.7 6.4 %collective-permute-start.7 = (bf16[16,512]{1,0:T(8,128)(2,1)S(1)}, bf16[16,512]{1,0:T(8,128)(2,1)S(1)}, u32[]{:S(2)}, u32[]{:S(2)}) collective-permute-start(bf16[16,512]{1,0:T(8,128)(2,1)S(1)} %collective-permute-done.6), channel_id=1, source_target_pairs={{0,4},{4,8},{8,12},{12,16},{16,20},{20,24},{24,28},{28,0},{1,5},{5... | collective-permute-start | bytes 49160 | tf_op jit(solution)/shard_map/ppermute | solution.py:12
  101.3 1.6 copy-start.1
  133.7 7.1 %copy-start = (f32[12,128,128]{2,1,0:T(8,128)S(1)}, f32[12,128,128]{2,1,0:T(8,128)}, u32[]{:S(2)}) copy-start(f32[12,128,128]{2,1,0:T(8,128)} %copy.128) | copy-start | bytes 2359300
  146.6 15.1 %copy-start.6 = (f32[16]{0:T(128)S(1)}, f32[16]{0:T(128)}, u32[]{:S(2)}) copy-start(f32[16]{0:T(128)} %add_sqrt_fusion) | copy-start | bytes 196
  186.4 5.0 %collective-permute-start.8 = (bf16[12,32,128]{2,0,1:T(8,128)(2,1)S(1)}, bf16[12,32,128]{2,0,1:T(8,128)(2,1)S(1)}, u32[]{:S(2)}, u32[]{:S(2)}) collective-permute-start(bf16[12,32,128]{2,0,1:T(8,128)(2,1)S(1)} %copy.144), channel_id=1, source_target_pairs={{0,4},{4,0},{8,12},{12,8},{16,20},{20,16},{24,28},{28,24},{1,5},{5... | collective-permute-start | bytes 294920 | tf_op jit(solution)/shard_map/ppermute | solution.py:25
